TPU v7x, 32 devices: a whole 2x2x4 slice. The times are simulated.
32 devices in a mesh: slab: 8 (over y, x, core), view: 4 (over z).
Axes of the slice: x: 2, y: 2, z: 4, core: 2. Of those that a mesh axis runs over, the one named last changes fastest.
Arguments:
- estimate: float32 [4, 1024, 1024], P(None, 'slab'), may hold values from 0.5 to 2
- views: float32 [4, 4, 1024, 1024], P('view', None, 'slab'), may hold values from 0.25 to 4
- psf: float32 [4, 1024, 1024], P('view', 'slab'), as said below
- pattern_mult: int32 [4, 8], P('view'), may hold values from 0 to 63
- pattern_shift: int32 [4, 8], P('view'), may hold values from 0 to 127
- interp: float32 [4, 8, 128], P('view'), may hold values from 0.05 to 0.45
Outputs:
- updated: float32 [4, 1024, 1024], P(None, 'slab')
Inputs may be any that keep to these rules, and one draw needn't show every extreme that they name: `psf`: every entry is positive.
All inputs are finite; a program needn't handle non-finite values.
Results may differ from a plain program's by a relative error of at most 0.0001.
Values sent between devices are 32-bit elements; how exact they have to be, the bound alone decides.
No kernel may reach another device: no remote copies, remote signals or barrier semaphores. Data moves between devices by JAX's collectives and lax.ppermute only.
A program may use at most 128 MiB of HBM per device.

v0:
```python
import math
import jax
import jax.numpy as jnp
from jax import lax
from jax.sharding import PartitionSpec as P

highest = lax.Precision.HIGHEST


def block_matrix(multiplier, shifting, weights):
    positions = jnp.arange(128, dtype=jnp.int32)
    first_col = ((2 * multiplier[:, None] + 1) * positions[None, :] + shifting[:, None]) % 128
    second_col = (first_col + 1) % 128
    columns = positions[None, None, :]
    lower = (columns == first_col[:, :, None]).astype(jnp.float32)
    upper = (columns == second_col[:, :, None]).astype(jnp.float32)
    return (1.0 - weights)[:, :, None] * lower + weights[:, :, None] * upper


def angle_tables(rows, cols, length):
    row_index = lax.iota(jnp.int32, rows)[:, None]
    col_index = lax.iota(jnp.int32, cols)[None, :]
    angles = (row_index * col_index % length).astype(jnp.float32) * (2.0 * math.pi / length)
    return (jnp.cos(angles), jnp.sin(angles))


def contract(form, real_part, imag_part, cosine, sine_table, direction, want_imag):
    real_cos = jnp.einsum(form, real_part, cosine, precision=highest)
    if imag_part is None:
        return (real_cos, direction * jnp.einsum(form, real_part, sine_table, precision=highest))
    imag_sin = jnp.einsum(form, imag_part, sine_table, precision=highest)
    out_real = real_cos - direction * imag_sin
    if not want_imag:
        return (out_real, None)
    real_sin = jnp.einsum(form, real_part, sine_table, precision=highest)
    imag_cos = jnp.einsum(form, imag_part, cosine, precision=highest)
    return (out_real, imag_cos + direction * real_sin)


def complex_times(real_part, imag_part, cosine, sine_table):
    return (
        real_part * cosine - imag_part * sine_table,
        real_part * sine_table + imag_part * cosine,
    )


def factored(real_part, imag_part, axis, direction, forward, want_imag):
    length = real_part.shape[axis]
    second = 128
    first = length // second
    if axis == 2:
        leading, trailing = ("rx", "")
    else:
        leading, trailing = ("r", "z")
    outer = real_part.shape
    shape = outer[:axis] + (first, second) + outer[axis + 1 :]
    real_part = real_part.reshape(shape)
    if imag_part is not None:
        imag_part = imag_part.reshape(shape)
    first_cos, first_sin = angle_tables(first, first, first)
    second_cos, second_sin = angle_tables(second, second, second)
    twist_cos, twist_sin = angle_tables(first, second, length)
    if axis == 1:
        twist_cos = twist_cos[:, :, None]
        twist_sin = twist_sin[:, :, None]
    twist_sin = direction * twist_sin
    if forward:
        real_part, imag_part = contract(
            leading + "ab" + trailing + ",ak->" + leading + "kb" + trailing,
            real_part,
            imag_part,
            first_cos,
            first_sin,
            direction,
            True,
        )
        real_part, imag_part = complex_times(real_part, imag_part, twist_cos, twist_sin)
        real_part, imag_part = contract(
            leading + "kb" + trailing + ",bm->" + leading + "km" + trailing,
            real_part,
            imag_part,
            second_cos,
            second_sin,
            direction,
            want_imag,
        )
    else:
        real_part, imag_part = contract(
            leading + "km" + trailing + ",mb->" + leading + "kb" + trailing,
            real_part,
            imag_part,
            second_cos,
            second_sin,
            direction,
            True,
        )
        real_part, imag_part = complex_times(real_part, imag_part, twist_cos, twist_sin)
        real_part, imag_part = contract(
            leading + "kb" + trailing + ",ka->" + leading + "ab" + trailing,
            real_part,
            imag_part,
            first_cos,
            first_sin,
            direction,
            want_imag,
        )
    real_part = real_part.reshape(outer)
    if imag_part is not None:
        imag_part = imag_part.reshape(outer)
    return (real_part, imag_part)


def to_columns(real_part, imag_part):
    depth_real, depth_imag = factored(real_part, imag_part, 2, -1.0, True, True)
    moved_real, moved_imag = (
        lax.all_to_all(depth_real, "slab", split_axis=2, concat_axis=1, tiled=True),
        lax.all_to_all(depth_imag, "slab", split_axis=2, concat_axis=1, tiled=True),
    )
    return factored(moved_real, moved_imag, 1, -1.0, True, True)


def to_planes(real_part, imag_part):
    width_real, width_imag = factored(real_part, imag_part, 1, 1.0, False, True)
    moved_real, moved_imag = (
        lax.all_to_all(width_real, "slab", split_axis=1, concat_axis=2, tiled=True),
        lax.all_to_all(width_imag, "slab", split_axis=1, concat_axis=2, tiled=True),
    )
    scaling = 1.0 / (width_real.shape[1] * moved_real.shape[2])
    out_real, out_imag = factored(moved_real, moved_imag, 2, 1.0, False, False)
    return (out_real * scaling, None)


def shards(estimate, views, psf, pattern_mult, pattern_shift, interp):
    row_count, slab_width, depth = estimate.shape
    blocks = block_matrix(pattern_mult[0], pattern_shift[0], interp[0])
    block_count = depth // 128
    shaped = estimate.reshape(row_count, slab_width, block_count, 128)
    sampled = jnp.einsum("bij,yxbj->yxbi", blocks, shaped, precision=highest).reshape(
        row_count, slab_width, depth
    )

    def pack(volume):
        return (volume, None)

    packed_real, packed_imag = pack(sampled)
    packed_real = jnp.concatenate([packed_real, psf], 0)
    spectra_real, spectra_imag = to_columns(packed_real, packed_imag)
    transfer_real = spectra_real[-1:]
    transfer_imag = spectra_imag[-1:]
    spectra_real = spectra_real[:-1]
    spectra_imag = spectra_imag[:-1]
    filtered_real = spectra_real * transfer_real - spectra_imag * transfer_imag
    filtered_imag = spectra_real * transfer_imag + spectra_imag * transfer_real
    blurred_real, blurred_imag = to_planes(filtered_real, filtered_imag)
    quotient = views[0] / blurred_real
    packed_real, packed_imag = pack(quotient)
    spectra_real, spectra_imag = to_columns(packed_real, packed_imag)
    filtered_real = spectra_real * transfer_real + spectra_imag * transfer_imag
    filtered_imag = spectra_imag * transfer_real - spectra_real * transfer_imag
    smeared_real, smeared_imag = to_planes(filtered_real, filtered_imag)
    correction = jnp.einsum(
        "bij,yxbi->yxbj",
        blocks,
        smeared_real.reshape(row_count, slab_width, block_count, 128),
        precision=highest,
    ).reshape(row_count, slab_width, depth)
    log_terms = jnp.log(correction)
    view_count = lax.axis_size("view")
    summed = lax.psum(log_terms, "view")
    return estimate * jnp.exp(summed / view_count)


def solution(mesh):
    placed = (
        P(None, "slab", None),
        P("view", None, "slab", None),
        P("view", "slab", None),
        P("view", None),
        P("view", None),
        P("view", None, None),
    )
    return jax.shard_map(
        shards, mesh=mesh, in_specs=placed, out_specs=P(None, "slab", None), check_vma=False
    )
```

profile of v0, /device:TPU:0, one launch (start us, length us, event | category | flops | bytes accessed | tf_op | source)
XLA Modules:
  0.0 555.8 jit_solution(18437681724977504398)
XLA Ops:
  10.0 3.6 fusion.121
  15.3 3.1 copy.145
  20.8 4.7 subtract_bitcast_fusion.2
  25.5 3.0 fusion.16
  28.6 3.2 multiply_add_fusion.1
  31.8 3.8 copy.157
  35.7 5.2 all-to-all-start.1
  40.8 3.0 fusion.18
  43.9 3.2 multiply_subtract_fusion.1
  47.1 3.6 copy.151
  50.7 39.3 %all-to-all-done.1 = f32[5,128,1024]{1,0,2:T(8,128)} async-done(((f32[5,128,1024]{1,0,2:T(8,128)}), f32[5,128,1024]{1,0,2:T(8,128)}, u32[]{:S(2)}, u32[]{:S(2)}) %all-to-all-start.1) | async-done | bytes 2621472 | tf_op jit(solution)/shard_map/all_to_all | solution.py:117
  90.0 4.8 all-to-all-start
  95.0 3.1 copy.268
  98.1 3.8 fusion
  101.9 3.9 fusion.2
  105.8 37.9 %all-to-all-done = f32[5,128,1024]{1,0,2:T(8,128)} async-done(((f32[5,128,1024]{1,0,2:T(8,128)}), f32[5,128,1024]{1,0,2:T(8,128)}, u32[]{:S(2)}, u32[]{:S(2)}) %all-to-all-start) | async-done | bytes 2621472 | tf_op jit(solution)/shard_map/all_to_all | solution.py:116
  143.7 3.1 copy.265
  146.8 4.3 multiply_add_fusion
  151.1 3.4 subtract_bitcast_fusion.1
  154.6 2.9 fusion.10
  157.4 2.9 fusion.8
  160.3 3.0 subtract_bitcast_fusion
  163.4 3.0 add_bitcast_fusion
  173.7 2.9 fusion.39
  176.7 3.3 fusion.77
  180.0 2.9 subtract_bitcast_fusion.6
  185.9 4.4 all-to-all-start.2
  190.3 4.5 fusion.75
  194.8 3.0 add_bitcast_fusion.6
  198.1 2.7 copy.181
  200.9 16.1 %all-to-all-done.2 = f32[4,1024,128]{2,0,1:T(4,128)} async-done(((f32[4,1024,128]{2,0,1:T(4,128)}), f32[4,1024,128]{2,0,1:T(4,128)}, u32[]{:S(2)}, u32[]{:S(2)}) %all-to-all-start.2) | async-done | bytes 2097184 | tf_op jit(solution)/shard_map/all_to_all | solution.py:125
  217.0 4.5 all-to-all-start.3
  225.1 3.4 fusion.171
  228.4 19.5 %all-to-all-done.3 = f32[4,1024,128]{2,0,1:T(4,128)} async-done(((f32[4,1024,128]{2,0,1:T(4,128)}), f32[4,1024,128]{2,0,1:T(4,128)}, u32[]{:S(2)}, u32[]{:S(2)}) %all-to-all-start.3) | async-done | bytes 2097184 | tf_op jit(solution)/shard_map/all_to_all | solution.py:126
  256.5 3.1 fusion.47
  259.6 3.3 bitcast_divide_fusion
  269.6 3.0 multiply_add_fusion.5
  275.3 4.4 all-to-all-start.5
  279.6 4.0 fusion.69
  286.3 2.7 copy.189
  289.0 17.3 %all-to-all-done.5 = f32[4,128,1024]{1,0,2:T(4,128)} async-done(((f32[4,128,1024]{1,0,2:T(4,128)}), f32[4,128,1024]{1,0,2:T(4,128)}, u32[]{:S(2)}, u32[]{:S(2)}) %all-to-all-start.5) | async-done | bytes 2097184 | tf_op jit(solution)/shard_map/all_to_all | solution.py:117
  306.3 4.5 all-to-all-start.4
  313.1 3.2 fusion.31
  316.3 3.2 fusion.33
  319.5 17.8 %all-to-all-done.4 = f32[4,128,1024]{1,0,2:T(4,128)} async-done(((f32[4,128,1024]{1,0,2:T(4,128)}), f32[4,128,1024]{1,0,2:T(4,128)}, u32[]{:S(2)}, u32[]{:S(2)}) %all-to-all-start.4) | async-done | bytes 2097184 | tf_op jit(solution)/shard_map/all_to_all | solution.py:116
  339.6 3.7 multiply_add_fusion.4
  360.5 2.8 convolution_subtract_fusion.1
  363.3 2.9 fusion.27
  366.2 2.9 fusion.53
  369.1 2.9 subtract_bitcast_fusion.3
  372.4 2.8 copy.214
  375.3 4.4 all-to-all-start.6
  379.6 4.5 fusion.51
  384.1 3.0 add_bitcast_fusion.3
  387.5 2.7 copy.219
  390.2 16.1 %all-to-all-done.6 = f32[4,1024,128]{2,0,1:T(4,128)} async-done(((f32[4,1024,128]{2,0,1:T(4,128)}), f32[4,1024,128]{2,0,1:T(4,128)}, u32[]{:S(2)}, u32[]{:S(2)}) %all-to-all-start.6) | async-done | bytes 2097184 | tf_op jit(solution)/shard_map/all_to_all | solution.py:125
  406.3 4.3 all-to-all-start.7
  412.6 3.4 fusion.167
  416.0 21.3 %all-to-all-done.7 = f32[4,1024,128]{2,0,1:T(4,128)} async-done(((f32[4,1024,128]{2,0,1:T(4,128)}), f32[4,1024,128]{2,0,1:T(4,128)}, u32[]{:S(2)}, u32[]{:S(2)}) %all-to-all-start.7) | async-done | bytes 2097184 | tf_op jit(solution)/shard_map/all_to_all | solution.py:126
  445.8 2.9 fusion.43
  448.7 3.3 multiply_bitcast_fusion
  457.7 84.9 %all-reduce.2.cloned.1.call-done = f32[4,128,1024]{1,2,0:T(8,128)} async-done(((f32[4,128,1024]{1,2,0:T(8,128)}), f32[4,128,1024]{1,2,0:T(8,128)}) %all-reduce.2.cloned.1.call-update) | async-done | bytes 2097168 | tf_op jit(solution)/shard_map/psum | solution.py:169
  542.6 3.2 exponential_multiply_fusion
  545.8 2.9 copy.226
  (76 shorter events, 81.1 us)
Async XLA Ops:
  18.4 2.4 copy-start
  25.5 3.1 copy-start.1
  35.7 54.4 %all-to-all-start.1 = ((f32[5,128,1024]{1,0,2:T(8,128)}), f32[5,128,1024]{1,0,2:T(8,128)}, u32[]{:S(2)}, u32[]{:S(2)}) async-start(f32[5,128,1024]{1,0,2:T(8,128)} %copy.157), calls=%async_computation.1 | async-start | bytes 8388608 | tf_op jit(solution)/shard_map/all_to_all | solution.py:117
  40.8 3.0 copy-start.2
  90.0 53.7 %all-to-all-start = ((f32[5,128,1024]{1,0,2:T(8,128)}), f32[5,128,1024]{1,0,2:T(8,128)}, u32[]{:S(2)}, u32[]{:S(2)}) async-start(f32[5,128,1024]{1,0,2:T(8,128)} %copy.151), calls=%async_computation | async-start | bytes 8388608 | tf_op jit(solution)/shard_map/all_to_all | solution.py:116
  146.8 4.3 copy-start.6
  176.7 3.3 copy-start.4
  185.9 31.0 %all-to-all-start.2 = ((f32[4,1024,128]{2,0,1:T(4,128)}), f32[4,1024,128]{2,0,1:T(4,128)}, u32[]{:S(2)}, u32[]{:S(2)}) async-start(f32[4,1024,128]{2,0,1:T(4,128)} %copy.176), calls=%async_computation.2 | async-start | bytes 4194304 | tf_op jit(solution)/shard_map/all_to_all | solution.py:125
  200.9 20.6 %copy-start.10 = (f32[1,4,128,1024]{3,2,1,0:T(8,128)S(1)}, f32[1,4,128,1024]{3,2,1,0:T(8,128)}, u32[]{:S(2)}) copy-start(f32[1,4,128,1024]{3,2,1,0:T(8,128)} %param.7) | copy-start | bytes 6291460
  217.0 31.0 %all-to-all-start.3 = ((f32[4,1024,128]{2,0,1:T(4,128)}), f32[4,1024,128]{2,0,1:T(4,128)}, u32[]{:S(2)}, u32[]{:S(2)}) async-start(f32[4,1024,128]{2,0,1:T(4,128)} %copy.181), calls=%async_computation.3 | async-start | bytes 4194304 | tf_op jit(solution)/shard_map/all_to_all | solution.py:126
  249.7 2.1 copy-start.7
  256.5 3.1 copy-start.11
  267.1 2.5 copy-start.5
  275.3 31.0 %all-to-all-start.5 = ((f32[4,128,1024]{1,0,2:T(4,128)}), f32[4,128,1024]{1,0,2:T(4,128)}, u32[]{:S(2)}, u32[]{:S(2)}) async-start(f32[4,128,1024]{1,0,2:T(4,128)} %copy.195), calls=%async_computation.5 | async-start | bytes 4194304 | tf_op jit(solution)/shard_map/all_to_all | solution.py:117
  306.3 31.0 %all-to-all-start.4 = ((f32[4,128,1024]{1,0,2:T(4,128)}), f32[4,128,1024]{1,0,2:T(4,128)}, u32[]{:S(2)}, u32[]{:S(2)}) async-start(f32[4,128,1024]{1,0,2:T(4,128)} %copy.189), calls=%async_computation.4 | async-start | bytes 4194304 | tf_op jit(solution)/shard_map/all_to_all | solution.py:116
  339.6 3.7 copy-start.9
  366.2 2.9 copy-start.3
  375.3 31.0 %all-to-all-start.6 = ((f32[4,1024,128]{2,0,1:T(4,128)}), f32[4,1024,128]{2,0,1:T(4,128)}, u32[]{:S(2)}, u32[]{:S(2)}) async-start(f32[4,1024,128]{2,0,1:T(4,128)} %copy.214), calls=%async_computation.6 | async-start | bytes 4194304 | tf_op jit(solution)/shard_map/all_to_all | solution.py:125
  406.3 31.0 %all-to-all-start.7 = ((f32[4,1024,128]{2,0,1:T(4,128)}), f32[4,1024,128]{2,0,1:T(4,128)}, u32[]{:S(2)}, u32[]{:S(2)}) async-start(f32[4,1024,128]{2,0,1:T(4,128)} %copy.219), calls=%async_computation.7 | async-start | bytes 4194304 | tf_op jit(solution)/shard_map/all_to_all | solution.py:126
  410.6 132.0 %all-reduce.2.cloned.1.call-start = ((), (), s32[]{:S(2)}) async-start(), calls=%async_computation.8 | async-start | bytes 4194304 | tf_op jit(solution)/shard_map/psum | solution.py:169
  439.0 2.1 copy-start.8
  448.7 3.3 copy-start.12
Sparse Core Ops, SparseCore 0:
  455.9 86.6 all-reduce.1
where the time goes:
time: 560 us; the launch traced here: 556 us
  waiting for transfers between devices  270 us (48%)
  matrix products  172 us (31%)
  local copies, waits for them, and re-layouts  55.7 us (10%)
  starting transfers between devices  36.6 us (7%)
  between operations  14.4 us (3%)
  other arithmetic  7.07 us (1%)
    psum x1, waiting for transfers between devices, shards(): summed = lax.psum(log_terms, 'view')  84.9 us
    all_to_all x2, waiting for transfers between devices, to_columns(): lax.all_to_all(depth_imag, 'slab', split_axis=2, concat_axis=1, tiled=True)  56.6 us
    all_to_all x2, waiting for transfers between devices, to_columns(): lax.all_to_all(depth_real, 'slab', split_axis=2, concat_axis=1, tiled=True)  55.7 us
    dot_general x16, matrix products, contract(): real_cos = jnp.einsum(form, real_part, cosine, precision=highest)  48.2 us
    dot_general x14, matrix products, contract(): imag_sin = jnp.einsum(form, imag_part, sine_table, precision=highest)  41.1 us
    all_to_all x2, waiting for transfers between devices, to_planes(): lax.all_to_all(width_imag, 'slab', split_axis=1, concat_axis=2, tiled=True)  40.8 us
    dot_general x12, matrix products, contract(): real_sin = jnp.einsum(form, real_part, sine_table, precision=highest)  36.4 us
    dot_general x12, matrix products, contract(): imag_cos = jnp.einsum(form, imag_part, cosine, precision=highest)  35.7 us
  transfers between devices with their start and end apart: 9, of which 9 were waited for; matrix products, arithmetic and copies ran while one was open for 13% of the time, Pallas kernels for 0%

commit v1 on v0

--- a/solution.py
+++ b/solution.py
@@ -166,7 +166,8 @@
     ).reshape(row_count, slab_width, depth)
     log_terms = jnp.log(correction)
     view_count = lax.axis_size("view")
-    summed = lax.psum(log_terms, "view")
+    terms = lax.all_gather(log_terms, "view")
+    summed = jnp.sum(terms, axis=0)
     return estimate * jnp.exp(summed / view_count)
 
 

time: 560 us -> 633 us (1.13)
  waiting for transfers between devices: 270 us -> 333 us
    all_gather x0 -> x1, waiting for transfers between devices: none -> 148 us  [shards(): terms = lax.all_gather(log_terms, 'view')]
    psum x1 -> x0, waiting for transfers between devices: 84.9 us -> none  [shards(): summed = lax.psum(log_terms, 'view')]
  transfers between devices with their start and end apart: 9 -> 9, of which waited for: 9 -> 9; matrix products, arithmetic and copies ran while one was open for 13% -> 12% of each run, Pallas kernels for 0% -> 0%
where the time goes in v1:
time: 633 us; the launch traced here: 628 us
  waiting for transfers between devices  333 us (53%)
  matrix products  172 us (27%)
  local copies, waits for them, and re-layouts  59.2 us (9%)
  starting transfers between devices  36.6 us (6%)
  between operations  14.4 us (2%)
  other arithmetic  13 us (2%)
    all_gather x1, waiting for transfers between devices, shards(): terms = lax.all_gather(log_terms, 'view')  148 us
    all_to_all x2, waiting for transfers between devices, to_columns(): lax.all_to_all(depth_imag, 'slab', split_axis=2, concat_axis=1, tiled=True)  56.6 us
    all_to_all x2, waiting for transfers between devices, to_columns(): lax.all_to_all(depth_real, 'slab', split_axis=2, concat_axis=1, tiled=True)  55.7 us
    dot_general x16, matrix products, contract(): real_cos = jnp.einsum(form, real_part, cosine, precision=highest)  48.2 us
    dot_general x14, matrix products, contract(): imag_sin = jnp.einsum(form, imag_part, sine_table, precision=highest)  41.1 us
    all_to_all x2, waiting for transfers between devices, to_planes(): lax.all_to_all(width_imag, 'slab', split_axis=1, concat_axis=2, tiled=True)  40.8 us
    dot_general x12, matrix products, contract(): real_sin = jnp.einsum(form, real_part, sine_table, precision=highest)  36.4 us
    dot_general x12, matrix products, contract(): imag_cos = jnp.einsum(form, imag_part, cosine, precision=highest)  35.7 us
  transfers between devices with their start and end apart: 9, of which 9 were waited for; matrix products, arithmetic and copies ran while one was open for 12% of the time, Pallas kernels for 0%

profile of v1, /device:TPU:0, one launch (start us, length us, event | category | flops | bytes accessed | tf_op | source)
XLA Modules:
  0.0 628.3 jit_solution(9787072392832856917)
XLA Ops:
  10.0 3.6 fusion.121
  15.3 3.1 copy.143
  20.8 4.7 subtract_bitcast_fusion.2
  25.5 3.0 fusion.16
  28.6 3.2 multiply_add_fusion.1
  31.8 3.8 copy.155
  35.7 5.2 all-to-all-start.1
  40.8 3.0 fusion.18
  43.9 3.2 multiply_subtract_fusion.1
  47.1 3.6 copy.149
  50.7 39.3 %all-to-all-done.1 = f32[5,128,1024]{1,0,2:T(8,128)} async-done(((f32[5,128,1024]{1,0,2:T(8,128)}), f32[5,128,1024]{1,0,2:T(8,128)}, u32[]{:S(2)}, u32[]{:S(2)}) %all-to-all-start.1) | async-done | bytes 2621472 | tf_op jit(solution)/shard_map/all_to_all | solution.py:117
  90.0 4.8 all-to-all-start
  95.0 3.1 copy.268
  98.1 3.8 fusion
  101.9 3.9 fusion.2
  105.8 37.9 %all-to-all-done = f32[5,128,1024]{1,0,2:T(8,128)} async-done(((f32[5,128,1024]{1,0,2:T(8,128)}), f32[5,128,1024]{1,0,2:T(8,128)}, u32[]{:S(2)}, u32[]{:S(2)}) %all-to-all-start) | async-done | bytes 2621472 | tf_op jit(solution)/shard_map/all_to_all | solution.py:116
  143.7 3.1 copy.265
  146.8 4.3 multiply_add_fusion
  151.1 3.4 subtract_bitcast_fusion.1
  154.6 2.9 fusion.10
  157.4 2.9 fusion.8
  160.3 3.0 subtract_bitcast_fusion
  163.4 3.0 add_bitcast_fusion
  173.7 2.9 fusion.39
  176.7 3.3 fusion.77
  180.0 2.9 subtract_bitcast_fusion.6
  185.9 4.4 all-to-all-start.2
  190.3 4.5 fusion.75
  194.8 3.0 add_bitcast_fusion.6
  198.1 2.7 copy.179
  200.9 16.1 %all-to-all-done.2 = f32[4,1024,128]{2,0,1:T(4,128)} async-done(((f32[4,1024,128]{2,0,1:T(4,128)}), f32[4,1024,128]{2,0,1:T(4,128)}, u32[]{:S(2)}, u32[]{:S(2)}) %all-to-all-start.2) | async-done | bytes 2097184 | tf_op jit(solution)/shard_map/all_to_all | solution.py:125
  217.0 4.5 all-to-all-start.3
  225.1 3.4 fusion.171
  228.4 19.5 %all-to-all-done.3 = f32[4,1024,128]{2,0,1:T(4,128)} async-done(((f32[4,1024,128]{2,0,1:T(4,128)}), f32[4,1024,128]{2,0,1:T(4,128)}, u32[]{:S(2)}, u32[]{:S(2)}) %all-to-all-start.3) | async-done | bytes 2097184 | tf_op jit(solution)/shard_map/all_to_all | solution.py:126
  256.5 3.1 fusion.47
  259.6 3.3 bitcast_divide_fusion
  269.6 3.0 multiply_add_fusion.5
  275.3 4.4 all-to-all-start.5
  279.6 4.0 fusion.69
  289.0 17.3 %all-to-all-done.5 = f32[4,128,1024]{1,0,2:T(4,128)} async-done(((f32[4,128,1024]{1,0,2:T(4,128)}), f32[4,128,1024]{1,0,2:T(4,128)}, u32[]{:S(2)}, u32[]{:S(2)}) %all-to-all-start.5) | async-done | bytes 2097184 | tf_op jit(solution)/shard_map/all_to_all | solution.py:117
  306.3 4.5 all-to-all-start.4
  313.1 3.2 fusion.31
  316.3 3.2 fusion.33
  319.5 17.8 %all-to-all-done.4 = f32[4,128,1024]{1,0,2:T(4,128)} async-done(((f32[4,128,1024]{1,0,2:T(4,128)}), f32[4,128,1024]{1,0,2:T(4,128)}, u32[]{:S(2)}, u32[]{:S(2)}) %all-to-all-start.4) | async-done | bytes 2097184 | tf_op jit(solution)/shard_map/all_to_all | solution.py:116
  339.6 3.7 multiply_add_fusion.4
  360.5 2.8 convolution_subtract_fusion.1
  363.3 2.9 fusion.27
  366.2 2.9 fusion.53
  369.1 2.9 subtract_bitcast_fusion.3
  372.4 2.8 copy.212
  375.3 4.4 all-to-all-start.6
  379.6 4.5 fusion.51
  384.1 3.0 add_bitcast_fusion.3
  390.2 16.1 %all-to-all-done.6 = f32[4,1024,128]{2,0,1:T(4,128)} async-done(((f32[4,1024,128]{2,0,1:T(4,128)}), f32[4,1024,128]{2,0,1:T(4,128)}, u32[]{:S(2)}, u32[]{:S(2)}) %all-to-all-start.6) | async-done | bytes 2097184 | tf_op jit(solution)/shard_map/all_to_all | solution.py:125
  406.3 4.3 all-to-all-start.7
  412.6 3.4 fusion.167
  416.0 21.3 %all-to-all-done.7 = f32[4,1024,128]{2,0,1:T(4,128)} async-done(((f32[4,1024,128]{2,0,1:T(4,128)}), f32[4,1024,128]{2,0,1:T(4,128)}, u32[]{:S(2)}, u32[]{:S(2)}) %all-to-all-start.7) | async-done | bytes 2097184 | tf_op jit(solution)/shard_map/all_to_all | solution.py:126
  445.8 2.9 fusion.43
  448.7 3.3 multiply_bitcast_fusion
  458.2 148.1 %all-gather.2.cloned.1.call-done = f32[4,4,128,1024]{3,2,1,0:T(8,128)} async-done(((f32[1,4,128,1024]{3,2,1,0:T(8,128)}), f32[4,4,128,1024]{3,2,1,0:T(8,128)}) %all-gather.2.cloned.1.call-update) | async-done | bytes 8388624 | tf_op jit(solution)/shard_map/all_gather | solution.py:169
  606.3 5.9 reduce_sum.9
  612.2 2.9 copy.287
  615.1 3.2 exponential_multiply_fusion
  618.3 2.9 copy.226
  (79 shorter events, 87.1 us)
Async XLA Ops:
  18.4 2.4 copy-start
  25.5 3.1 copy-start.1
  35.7 54.4 %all-to-all-start.1 = ((f32[5,128,1024]{1,0,2:T(8,128)}), f32[5,128,1024]{1,0,2:T(8,128)}, u32[]{:S(2)}, u32[]{:S(2)}) async-start(f32[5,128,1024]{1,0,2:T(8,128)} %copy.155), calls=%async_computation.1 | async-start | bytes 8388608 | tf_op jit(solution)/shard_map/all_to_all | solution.py:117
  40.8 3.0 copy-start.2
  90.0 53.7 %all-to-all-start = ((f32[5,128,1024]{1,0,2:T(8,128)}), f32[5,128,1024]{1,0,2:T(8,128)}, u32[]{:S(2)}, u32[]{:S(2)}) async-start(f32[5,128,1024]{1,0,2:T(8,128)} %copy.149), calls=%async_computation | async-start | bytes 8388608 | tf_op jit(solution)/shard_map/all_to_all | solution.py:116
  146.8 4.3 copy-start.6
  176.7 3.3 copy-start.4
  185.9 31.0 %all-to-all-start.2 = ((f32[4,1024,128]{2,0,1:T(4,128)}), f32[4,1024,128]{2,0,1:T(4,128)}, u32[]{:S(2)}, u32[]{:S(2)}) async-start(f32[4,1024,128]{2,0,1:T(4,128)} %copy.174), calls=%async_computation.2 | async-start | bytes 4194304 | tf_op jit(solution)/shard_map/all_to_all | solution.py:125
  200.9 20.6 %copy-start.10 = (f32[1,4,128,1024]{3,2,1,0:T(8,128)S(1)}, f32[1,4,128,1024]{3,2,1,0:T(8,128)}, u32[]{:S(2)}) copy-start(f32[1,4,128,1024]{3,2,1,0:T(8,128)} %param.7) | copy-start | bytes 6291460
  217.0 31.0 %all-to-all-start.3 = ((f32[4,1024,128]{2,0,1:T(4,128)}), f32[4,1024,128]{2,0,1:T(4,128)}, u32[]{:S(2)}, u32[]{:S(2)}) async-start(f32[4,1024,128]{2,0,1:T(4,128)} %copy.179), calls=%async_computation.3 | async-start | bytes 4194304 | tf_op jit(solution)/shard_map/all_to_all | solution.py:126
  249.7 2.1 copy-start.7
  256.5 3.1 copy-start.11
  267.1 2.5 copy-start.5
  275.3 31.0 %all-to-all-start.5 = ((f32[4,128,1024]{1,0,2:T(4,128)}), f32[4,128,1024]{1,0,2:T(4,128)}, u32[]{:S(2)}, u32[]{:S(2)}) async-start(f32[4,128,1024]{1,0,2:T(4,128)} %copy.193), calls=%async_computation.5 | async-start | bytes 4194304 | tf_op jit(solution)/shard_map/all_to_all | solution.py:117
  306.3 31.0 %all-to-all-start.4 = ((f32[4,128,1024]{1,0,2:T(4,128)}), f32[4,128,1024]{1,0,2:T(4,128)}, u32[]{:S(2)}, u32[]{:S(2)}) async-start(f32[4,128,1024]{1,0,2:T(4,128)} %copy.187), calls=%async_computation.4 | async-start | bytes 4194304 | tf_op jit(solution)/shard_map/all_to_all | solution.py:116
  339.6 3.7 copy-start.9
  366.2 2.9 copy-start.3
  375.3 31.0 %all-to-all-start.6 = ((f32[4,1024,128]{2,0,1:T(4,128)}), f32[4,1024,128]{2,0,1:T(4,128)}, u32[]{:S(2)}, u32[]{:S(2)}) async-start(f32[4,1024,128]{2,0,1:T(4,128)} %copy.212), calls=%async_computation.6 | async-start | bytes 4194304 | tf_op jit(solution)/shard_map/all_to_all | solution.py:125
  406.3 31.0 %all-to-all-start.7 = ((f32[4,1024,128]{2,0,1:T(4,128)}), f32[4,1024,128]{2,0,1:T(4,128)}, u32[]{:S(2)}, u32[]{:S(2)}) async-start(f32[4,1024,128]{2,0,1:T(4,128)} %copy.217), calls=%async_computation.7 | async-start | bytes 4194304 | tf_op jit(solution)/shard_map/all_to_all | solution.py:126
  410.6 195.7 %all-gather.2.cloned.1.call-start = ((), (), s32[]{:S(2)}) async-start(), calls=%async_computation.8 | async-start | bytes 10485760 | tf_op jit(solution)/shard_map/all_gather | solution.py:169
  439.0 2.1 copy-start.8
  448.7 3.3 copy-start.12
Sparse Core Ops, SparseCore 0:
  456.4 149.8 all-gather.1
